TPU v7x, 32 devices: a whole 2x2x4 slice. The times are simulated.
32 devices in a mesh: groups: 2 (over y), pipe: 4 (over z), dp: 2 (over x), mp: 2 (over core).
Axes of the slice: x: 2, y: 2, z: 4, core: 2. Of those that a mesh axis runs over, the one named last changes fastest.
Arguments:
- latent: bfloat16 [4, 2, 2, 4, 16, 320], P(('groups', 'dp')), parts along dimension 0, may hold values from -6 to 6
- section_weight: bfloat16 [4, 2, 921600], P('pipe', None, 'mp'), may hold values from -0.01613743 to 0.01613743, as said below
- out_grad: bfloat16 [4, 2, 2, 4, 16, 320], P(('groups', 'dp')), parts along dimension 0, may hold values from -0.29882812 to 0.29882812
Outputs:
- section_grad: float32 [8, 921600], P(('groups', 'pipe'), 'mp'), parts along dimension 0
There are 2 independent parts, one for each index of `groups`. A program takes and returns all parts, laid end to end along the dimension named above; an argument that names none is the same for every part. Nothing has to cross between parts.
Inputs may be any that keep to these rules, and one draw needn't show every extreme that they name: section_weight[j, 0] equals section_weight[3 - j, 0] and section_weight[j, 1] equals section_weight[3 - j, 1] for every j: both devices of a mirrored pair hold the same two blocks.
All inputs are finite; a program needn't handle non-finite values.
Results may differ from a plain program's by a relative error of at most 0.0065.
Values may be sent and summed in bfloat16 or wider, within the bound.
No kernel may reach another device: no remote copies, remote signals or barrier semaphores. Data moves between devices by JAX's collectives and lax.ppermute only.
A program may use at most 64 MiB of HBM per device.

v0:
```python
import jax
import jax.numpy as jnp
from jax import lax
from jax.sharding import PartitionSpec as P


def silu_slope(pre_act):
    sigmoid = jax.nn.sigmoid(pre_act)
    return sigmoid * (1.0 + pre_act * (1.0 - sigmoid))


def conv(act, weight):
    return lax.conv_general_dilated(
        act,
        weight,
        (1, 1),
        ((1, 1), (1, 1)),
        dimension_numbers=("NHWC", "OHWI", "NHWC"),
        preferred_element_type=jnp.float32,
    )


def conv_t(cot, weight):
    flipped = jnp.flip(cot, (1, 2))
    out = lax.conv_general_dilated(
        flipped,
        weight,
        (1, 1),
        ((1, 1), (1, 1)),
        dimension_numbers=("NHWC", "IHWO", "NHWC"),
        preferred_element_type=jnp.float32,
    )
    return jnp.flip(out, (1, 2))


def conv_flipped(flipped, weight):
    return lax.conv_general_dilated(
        flipped,
        weight,
        (1, 1),
        ((1, 1), (1, 1)),
        dimension_numbers=("NHWC", "IHWO", "NHWC"),
        preferred_element_type=jnp.float32,
    )


def weight_grad(act, cot):
    return lax.conv_general_dilated(
        act,
        cot,
        (1, 1),
        ((1, 1), (1, 1)),
        dimension_numbers=("CHWN", "IHWO", "CHWN"),
        preferred_element_type=jnp.float32,
    )


def f32(v):
    return v.astype(jnp.float32)


def bf16(v):
    return v.astype(jnp.bfloat16)


def on_stage(active, fn, *args):
    shapes = jax.eval_shape(fn, *args)

    def idle(*unused):
        return jax.tree.map(lambda v: jnp.zeros(v.shape, v.dtype), shapes)

    return lax.cond(active, fn, idle, *args)


def local(latent, section_weight, out_grad):
    pipe_size = lax.axis_size("pipe")
    half = pipe_size // 2
    device = lax.axis_index("pipe")
    lower = device < half
    stage = jnp.minimum(device, pipe_size - 1 - device)
    lane = lax.axis_index("mp")
    swap = [(0, 1), (1, 0)]
    channels = latent.shape[-1]
    img = latent.shape[-3:]
    samples = latent.reshape((-1,) + img)
    grads = out_grad.reshape((-1,) + img)
    per_lane = samples.shape[0] // 2
    mine = lane * per_lane
    theirs = (1 - lane) * per_lane
    chan_half = section_weight.shape[-1] // (9 * channels)
    own = lax.optimization_barrier(
        section_weight[0]
        .reshape(2, chan_half, 9, channels)
        .transpose(0, 2, 1, 3)
        .reshape(2, 3, 3, chan_half, channels)
    ).transpose(0, 3, 1, 2, 4)
    other = lax.ppermute(own, "mp", swap)

    def up(t, v):
        pairs = [(t, t + 1), (pipe_size - 1 - t, pipe_size - 2 - t)]
        return lax.ppermute(v, "pipe", pairs)

    def down(t, v):
        pairs = [(t, t - 1), (pipe_size - 1 - t, pipe_size - t)]
        return lax.ppermute(v, "pipe", pairs)

    def take(v, at):
        return lax.dynamic_slice_in_dim(v, at, per_lane, 0)

    def join(first, second):
        return jnp.where(
            lane == 0, jnp.concatenate([first, second], -1), jnp.concatenate([second, first], -1)
        )

    low = lane * chan_half
    high = (1 - lane) * chan_half
    x0 = take(samples, mine)
    seed = take(grads, mine)
    a0 = bf16(jax.nn.silu(f32(x0)))

    def first_own(a0, seed, own):
        flipped = jnp.flip(seed, (1, 2))
        d_own = conv_flipped(lax.dynamic_slice_in_dim(flipped, low, chan_half, 3), own[1])
        return (conv(a0, own[0]), d_own)

    def first_h1(x0, a0, other_enc, h1_own):
        return bf16(f32(x0) + join(h1_own, conv(a0, other_enc)))

    def first_d(seed, other_dec, d_own):
        flipped = jnp.flip(seed, (1, 2))
        d_other = conv_flipped(lax.dynamic_slice_in_dim(flipped, high, chan_half, 3), other_dec)
        return jnp.flip(d_own + d_other, (1, 2))

    h1_own, d_own = on_stage(stage == 0, first_own, a0, seed, own)
    h1 = on_stage(stage == 0, first_h1, x0, a0, other[0], h1_own)
    h1_r = up(0, h1)
    d_last = on_stage(stage == 0, first_d, seed, other[1], d_own)
    d_last_r = up(0, d_last)
    other, _ = lax.optimization_barrier((other, h1))
    full = jnp.where(lane == 0, jnp.concatenate([own, other], 1), jnp.concatenate([other, own], 1))
    w_enc, w_dec = (full[0], full[1])
    enc_in, enc_act, enc_out = ({}, {}, {})
    enc_in[0], enc_act[0], enc_out[0] = (x0, a0, h1)
    received = h1_r
    for t in range(1, half):
        h_in = received
        u = f32(h_in)
        a = bf16(jax.nn.silu(u))
        h_out = bf16(u + conv(a, w_enc))
        enc_in[t], enc_act[t], enc_out[t] = (h_in, a, h_out)
        if t < half - 1:
            received = up(t, h_out)
    dec_u, dec_act, dec_c = ({}, {}, {})
    h_in = enc_out[half - 1]
    u = f32(h_in) + f32(h_in)
    a = bf16(jax.nn.silu(u))
    current = bf16(f32(h_in) + conv(a, w_dec))
    dec_u[half - 1], dec_act[half - 1] = (u, a)
    for t in range(half - 2, 0, -1):
        h_in = down(t + 1, current)
        u = f32(h_in) + f32(enc_out[t])
        a = bf16(jax.nn.silu(u))
        current = bf16(f32(h_in) + conv(a, w_dec))
        dec_u[t], dec_act[t] = (u, a)
    u_last = f32(current) + f32(h1_r)
    a_last = bf16(jax.nn.silu(u_last))
    b_last = d_last_r * silu_slope(u_last)
    skip = {1: bf16(b_last)}
    cot = bf16(f32(seed) + b_last)
    for t in range(1, half):
        if t > 1:
            cot = up(t - 1, cot)
        dec_c[t] = cot
        d = conv_t(cot, w_dec)
        b = d * silu_slope(dec_u[t])
        g = bf16(f32(cot) + b)
        if t < half - 1:
            skip[t + 1] = bf16(b)
            cot = g
        else:
            cot = bf16(f32(g) + b)
    enc_c = {}
    for t in range(half - 1, 0, -1):
        if t < half - 1:
            cot = bf16(f32(down(t + 1, cot)) + f32(skip[t + 1]))
        enc_c[t] = cot
        d = conv_t(cot, w_enc)
        b = d * silu_slope(f32(enc_in[t]))
        cot = bf16(f32(cot) + b)
    c0 = bf16(f32(cot) + f32(skip[1]))
    sent = lax.ppermute(
        jnp.where(lower, c0, a_last), "pipe", [(1, 0), (pipe_size - 2, pipe_size - 1)]
    )
    acts_lo = jnp.stack([a0] + [enc_act[t] for t in range(1, half)])
    cots_lo = jnp.stack([sent] + [enc_c[t] for t in range(1, half)])
    acts_up = jnp.stack([sent] + [dec_act[t] for t in range(1, half)])
    cots_up = jnp.stack([seed] + [dec_c[t] for t in range(1, half)])
    act_sel = jnp.where(lower, acts_lo[stage], acts_up[stage])
    cot_sel = jnp.where(lower, cots_lo[stage], cots_up[stage])
    both = jnp.concatenate([act_sel, cot_sel], axis=-1)
    every = lax.all_gather(both, ("dp", "mp"), axis=0, tiled=True)
    act_all = every[..., :channels]
    cot_all = lax.dynamic_slice_in_dim(every, channels + low, chan_half, 3)
    grad = weight_grad(act_all, cot_all)
    return grad.reshape(1, -1)


def solution(mesh):
    return jax.shard_map(
        local,
        mesh=mesh,
        in_specs=(
            P(("groups", "dp"), None, None, None, None, None),
            P("pipe", None, "mp"),
            P(("groups", "dp"), None, None, None, None, None),
        ),
        out_specs=P(("groups", "pipe"), "mp"),
        check_vma=False,
    )
```

profile of v0, /device:TPU:0, one launch (start us, length us, event | category | flops | bytes accessed | tf_op | source)
XLA Modules:
  0.0 60.7 jit_solution(1006946981016055921)
XLA Ops:
  0.0 2.7 %reshape.100 = bf16[921600]{0:T(1024)(128)(2,1)S(1)} reshape(bf16[1,2,460800]{2,1,0:T(2,128)(2,1)} %param.10) | data formatting | bytes 3686400
  2.7 4.5 %reshape_squeeze.3 = bf16[2,160,9,320]{3,2,1,0:T(8,128)(2,1)} reshape(bf16[921600]{0:T(1024)(128)(2,1)S(1)} %reshape.100) | data formatting | bytes 3686400 | tf_op jit(solution)/shard_map/reshape;squeeze | solution.py:93
  7.1 2.7 %copy.72 = bf16[2,9,160,320]{3,2,1,0:T(8,128)(2,1)S(1)} copy(bf16[2,9,160,320]{3,1,2,0:T(8,128)(2,1)} %bitcast.129) | data formatting | bytes 3686400 | tf_op jit(solution)/shard_map/transpose | solution.py:94
  9.8 0.5 collective-permute-start
  10.6 0.1 fusion.67
  10.7 2.6 %conditional.3 = (f32[2,4,16,160]{3,1,2,0:T(4,128)S(1)}, f32[2,4,16,320]{3,1,2,0:T(4,128)S(1)}) conditional(s32[]{:T(128)} %convert_element_type.83, () %tuple.30, (bf16[2,160,3,3,320]{4,1,3,2,0:T(8,128)(2,1)S(1)}, bf16[2,4,16,320]{3,1,2,0:T(4,128)(2,1)S(1)}, bf16[2,4,16,320]{3,1,2,0:T(4,128)(2,1)S(1)}, s32[]{:T(128)}) %tuple.54), branch_computations={%region_0.1_spmd, %region_1.2_spmd} | conditional | flops 295925760 | bytes 5914902 | solution.py:72
  10.9 0.2 dynamic-slice_bitcast_fusion
  11.2 0.2 fusion.7
  11.7 0.2 fusion.4
  11.9 0.5 convolution_select_fusion.1
  12.5 0.5 convolution_select_fusion
  13.0 0.1 copy.66
  13.1 0.1 copy.64
  13.3 1.1 %collective-permute-done = bf16[2,160,3,3,320]{4,1,3,2,0:T(8,128)(2,1)} collective-permute-done((bf16[2,160,3,3,320]{4,1,3,2,0:T(8,128)(2,1)S(1)}, bf16[2,160,3,3,320]{4,1,3,2,0:T(8,128)(2,1)}, u32[]{:S(2)}, u32[]{:S(2)}) %collective-permute-start) | collective-permute-done | bytes 1843232 | tf_op jit(solution)/shard_map/ppermute | solution.py:97
  14.4 2.7 %conditional.4 = (bf16[2,4,16,320]{3,1,2,0:T(4,128)(2,1)S(1)}) conditional(s32[]{:T(128)} %convert_element_type.83, () %tuple.29, (bf16[2,4,16,320]{3,1,2,0:T(4,128)(2,1)S(1)}, s32[]{:T(128)}, bf16[2,160,3,3,320]{4,1,3,2,0:T(8,128)(2,1)}, bf16[2,4,16,320]{3,1,2,0:T(4,128)(2,1)S(1)}, f32[2,4,16,160]{3,1,2,0:T(4,128)S(1)}) %tuple.32), branch_computations={%region_2.3_spmd, %region_3.4_spmd} | conditional | flops 148346880 | bytes 3082772 | solution.py:72
  14.7 0.2 fusion.12
  14.9 1.8 %convolution_select_fusion.2 = f32[4,16,3,160]{3,1,2,0:T(8,128)S(1)} fusion(bf16[2,160,3,3,320]{4,1,3,2,0:T(8,128)(2,1)} %get-tuple-element.63, bf16[4,2,8,5,320]{4,1,3,2,0:T(2,128)(2,1)S(1)} %fusion.12, pred[16,3]{0,1:T(4,128)(4,1)} %constant.95), kind=kOutput, calls=%fused_computation.18 | convolution fusion | flops 147486720 | bytes 1434112 | tf_op jit(solution)/shard_map/cond/branch_1_fun/conv_general_dilated | solution.py:13
  16.7 0.1 copy.68
  16.9 0.2 fusion.16
  17.1 2.2 %collective-permute-start.1 = (bf16[2,4,16,320]{3,1,2,0:T(4,128)(2,1)S(1)}, bf16[2,4,16,320]{3,1,2,0:T(4,128)(2,1)S(1)}, u32[]{:S(2)}, u32[]{:S(2)}) collective-permute-start(bf16[2,4,16,320]{3,1,2,0:T(4,128)(2,1)S(1)} %get-tuple-element.119), channel_id=1, source_target_pairs={{0,4},{12,8},{1,5},{13,9},{2,6},{14,10},{3,7},{15,11},{16,20},{28,... | collective-permute-start | bytes 245768 | tf_op jit(solution)/shard_map/ppermute | solution.py:101
  19.3 3.0 %conditional.5 = (f32[2,4,16,320]{3,1,2,0:T(4,128)S(1)}) conditional(s32[]{:T(128)} %convert_element_type.83, () %tuple.33, (bf16[2,4,16,320]{3,1,2,0:T(4,128)(2,1)S(1)}, s32[]{:T(128)}, bf16[2,160,3,3,320]{4,1,3,2,0:T(8,128)(2,1)}, f32[2,4,16,320]{3,1,2,0:T(4,128)S(1)}) %tuple.34), branch_computations={%region_4.5_spmd, %region_5.6_spmd} | conditional | flops 147865600 | bytes 3548744 | solution.py:72
  19.5 0.1 dynamic-slice_bitcast_fusion.1
  19.8 0.2 fusion.20
  20.0 1.8 %convolution_select_fusion.3 = f32[4,16,3,320]{3,1,2,0:T(8,128)S(1)} fusion(bf16[2,160,3,3,320]{4,1,3,2,0:T(8,128)(2,1)} %get-tuple-element.67, bf16[4,2,8,5,160]{4,1,3,2,0:T(2,128)(2,1)S(1)} %fusion.20, pred[16,3]{0,1:T(4,128)(4,1)} %constant.94), kind=kOutput, calls=%fused_computation.30 | convolution fusion | flops 147517440 | bytes 1454592 | tf_op jit(solution)/shard_map/cond/branch_1_fun/conv_general_dilated | solution.py:37
  22.0 0.3 rev.20
  22.3 1.5 %collective-permute-start.2 = (f32[2,4,16,320]{3,1,2,0:T(4,128)S(1)}, f32[2,4,16,320]{3,1,2,0:T(4,128)S(1)}, u32[]{:S(2)}, u32[]{:S(2)}) collective-permute-start(f32[2,4,16,320]{3,1,2,0:T(4,128)S(1)} %get-tuple-element.120), channel_id=1, source_target_pairs={{0,4},{12,8},{1,5},{13,9},{2,6},{14,10},{3,7},{15,11},{16,20},{28,... | collective-permute-start | bytes 491528 | tf_op jit(solution)/shard_map/ppermute | solution.py:101
  23.8 3.6 %maximum_select_fusion.1 = bf16[2,320,3,3,320]{4,1,3,2,0:T(8,128)(2,1)S(1)} fusion(bf16[2,160,3,3,320]{4,1,3,2,0:T(8,128)(2,1)} %collective-permute-done, bf16[2,160,3,3,320]{4,1,3,2,0:T(8,128)(2,1)S(1)} %bitcast.132, pred[]{:T(512)S(6)} %eq.12), kind=kLoop, calls=%fused_computation.40 | loop fusion | flops 16588800 | bytes 7372801 | tf_op jit(solution)/shard_map/jit(_where)/select_n | solution.py:140
  27.7 1.0 %fusion.29 = f32[4,16,3,320]{3,1,2,0:T(8,128)S(1)} fusion(bf16[2,320,3,3,320]{4,1,3,2,0:T(8,128)(2,1)S(1)} %maximum_select_fusion.1, bf16[4,2,7,2,320]{4,2,1,3,0:T(8,128)(2,1)S(1)} %slice.51, bf16[4,2,8,3,320]{4,2,1,3,0:T(8,128)(2,1)S(1)} %copy.79, pred[16,3]{0,1:T(4,128)(4,1)S(1)} %copy-done.3), kind=kOutput, calls=%fused_computation.49 | convolution fusion | flops 295587840 | bytes 2703872 | tf_op jit(solution)/shard_map/conv_general_dilated | solution.py:13
  28.8 0.1 fusion.71
  29.1 1.0 %fusion.27 = f32[4,16,3,320]{3,1,2,0:T(8,128)S(1)} fusion(bf16[2,320,3,3,320]{4,1,3,2,0:T(8,128)(2,1)S(1)} %maximum_select_fusion.1, bf16[4,2,7,2,320]{4,2,1,3,0:T(8,128)(2,1)S(1)} %slice.54, bf16[4,2,8,3,320]{4,2,1,3,0:T(8,128)(2,1)S(1)} %copy.82, pred[16,3]{0,1:T(4,128)(4,1)S(1)} %copy-done.3), kind=kOutput, calls=%fused_computation.47 | convolution fusion | flops 295587840 | bytes 2703872 | tf_op jit(solution)/shard_map/conv_general_dilated | solution.py:13
  30.3 0.2 add_convert_fusion.3
  30.5 0.3 rev.25
  30.9 2.4 %fusion.28 = f32[4,16,3,320]{3,1,2,0:T(8,128)S(1)} fusion(bf16[2,320,3,3,320]{4,1,3,2,0:T(8,128)(2,1)} %copy-done, bf16[4,2,7,2,320]{4,2,1,3,0:T(8,128)(2,1)S(1)} %slice.57, bf16[4,2,8,3,320]{4,2,1,3,0:T(8,128)(2,1)S(1)} %copy.85, pred[16,3]{0,1:T(4,128)(4,1)S(1)} %copy-done.3), kind=kOutput, calls=%fused_computation.48 | convolution fusion | flops 295587840 | bytes 2652208 | tf_op jit(solution)/shard_map/conv_general_dilated | solution.py:25
  33.5 0.3 rev.26
  33.8 0.2 add_convert_fusion.1
  34.0 0.3 rev.27
  34.5 2.4 %fusion.30 = f32[4,16,3,320]{3,1,2,0:T(8,128)S(1)} fusion(bf16[2,320,3,3,320]{4,1,3,2,0:T(8,128)(2,1)} %copy-done, bf16[4,2,7,2,320]{4,2,1,3,0:T(8,128)(2,1)S(1)} %slice.59, bf16[4,2,8,3,320]{4,2,1,3,0:T(8,128)(2,1)S(1)} %copy.88, pred[16,3]{0,1:T(4,128)(4,1)S(1)} %copy-done.3), kind=kOutput, calls=%fused_computation.50 | convolution fusion | flops 295587840 | bytes 2652208 | tf_op jit(solution)/shard_map/conv_general_dilated | solution.py:25
  37.0 0.3 rev.28
  37.3 0.3 fusion.90
  37.7 1.3 %collective-permute-start.3 = (bf16[2,4,16,320]{3,1,2,0:T(4,128)(2,1)S(1)}, bf16[2,4,16,320]{3,1,2,0:T(4,128)(2,1)S(1)}, u32[]{:S(2)}, u32[]{:S(2)}) collective-permute-start(bf16[2,4,16,320]{3,1,2,0:T(4,128)(2,1)S(1)} %fusion.90), channel_id=1, source_target_pairs={{4,0},{8,12},{5,1},{9,13},{6,2},{10,14},{7,3},{11,15},{20,16},{24,... | collective-permute-start | bytes 245768 | tf_op jit(solution)/shard_map/ppermute | solution.py:191
  39.1 5.1 %collective-permute-done.3 = bf16[2,4,16,320]{3,1,2,0:T(4,128)(2,1)S(1)} collective-permute-done((bf16[2,4,16,320]{3,1,2,0:T(4,128)(2,1)S(1)}, bf16[2,4,16,320]{3,1,2,0:T(4,128)(2,1)S(1)}, u32[]{:S(2)}, u32[]{:S(2)}) %collective-permute-start.3) | collective-permute-done | bytes 81952 | tf_op jit(solution)/shard_map/ppermute | solution.py:191
  44.2 0.4 fusion.97
  44.6 0.1 pad_maximum_fusion
  44.8 8.8 %all_gather.3 = bf16[8,4,16,640]{3,2,1,0:T(8,128)(2,1)S(1)} all-gather(bf16[2,4,16,640]{3,2,1,0:T(8,128)(2,1)S(1)} %copy.90), channel_id=1, replica_groups=mesh['groups'=2,'pipe'=4,'dp'=2,'mp'=2] {'dp','mp'}, dimensions={0}, use_global_device_ids=true | all-gather | bytes 819200 | tf_op jit(solution)/shard_map/all_gather | solution.py:201
  53.6 0.2 constant_dynamic-slice_fusion
  53.8 0.9 %fusion.35 = f32[160,3,3,320]{3,0,2,1:T(8,128)S(1)} fusion(bf16[8,4,16,320]{3,2,1,0:T(8,128)(2,1)S(1)} %slice.61, bf16[8,4,16,160]{3,2,1,0:T(8,128)(2,1)S(1)} %constant_dynamic-slice_fusion), kind=kOutput, calls=%fused_computation.56 | convolution fusion | flops 376832000 | bytes 2334720 | tf_op jit(solution)/shard_map/conv_general_dilated | solution.py:48
  54.6 1.5 %copy.93 = f32[160,3,3,320]{3,2,1,0:T(4,128)S(1)} copy(f32[160,3,3,320]{3,0,2,1:T(8,128)S(1)} %fusion.35) | data formatting | bytes 3686400 | tf_op jit(solution)/shard_map/conv_general_dilated | solution.py:48
  56.2 4.6 %reshape.19 = f32[1,460800]{1,0:T(1,128)} reshape(f32[160,3,3,320]{3,2,1,0:T(4,128)S(1)} %copy.93) | data formatting | bytes 3686400 | tf_op jit(solution)/shard_map/reshape | solution.py:205
  (57 shorter events, 2.8 us)
Async XLA Ops:
  7.1 3.2 %copy-start.1 = (bf16[1,2,2,4,16,320]{5,4,3,2,1,0:T(8,128)(2,1)S(1)}, bf16[1,2,2,4,16,320]{5,4,3,2,1,0:T(8,128)(2,1)}, u32[]{:S(2)}) copy-start(bf16[1,2,2,4,16,320]{5,4,3,2,1,0:T(8,128)(2,1)} %param.9) | copy-start | bytes 491524
  7.1 3.3 %copy-start.2 = (bf16[1,2,2,4,16,320]{5,4,3,2,1,0:T(8,128)(2,1)S(1)}, bf16[1,2,2,4,16,320]{5,4,3,2,1,0:T(8,128)(2,1)}, u32[]{:S(2)}) copy-start(bf16[1,2,2,4,16,320]{5,4,3,2,1,0:T(8,128)(2,1)} %param.11) | copy-start | bytes 491524
  9.8 4.6 %collective-permute-start = (bf16[2,160,3,3,320]{4,1,3,2,0:T(8,128)(2,1)S(1)}, bf16[2,160,3,3,320]{4,1,3,2,0:T(8,128)(2,1)}, u32[]{:S(2)}, u32[]{:S(2)}) collective-permute-start(bf16[2,160,3,3,320]{4,1,3,2,0:T(8,128)(2,1)S(1)} %bitcast.130), channel_id=1, source_target_pairs={{0,1},{1,0},{2,3},{3,2},{4,5},{5,4},{6,7},{7,6},{8,9},{9,8},{10,11... | collective-permute-start | bytes 5529608 | tf_op jit(solution)/shard_map/ppermute | solution.py:97
  10.7 1.2 %copy-start.4 = (pred[16,3]{0,1:T(4,128)(4,1)S(1)}, pred[16,3]{0,1:T(4,128)(4,1)}, u32[]{:S(2)}) copy-start(pred[16,3]{0,1:T(4,128)(4,1)} %constant.96) | copy-start | bytes 148 | tf_op jit(solution)/shard_map/cond
  17.1 10.3 %collective-permute-start.1 = (bf16[2,4,16,320]{3,1,2,0:T(4,128)(2,1)S(1)}, bf16[2,4,16,320]{3,1,2,0:T(4,128)(2,1)S(1)}, u32[]{:S(2)}, u32[]{:S(2)}) collective-permute-start(bf16[2,4,16,320]{3,1,2,0:T(4,128)(2,1)S(1)} %get-tuple-element.119), channel_id=1, source_target_pairs={{0,4},{12,8},{1,5},{13,9},{2,6},{14,10},{3,7},{15,11},{16,20},{28,... | collective-permute-start | bytes 245768 | tf_op jit(solution)/shard_map/ppermute | solution.py:101
  22.3 5.4 %copy-start.3 = (pred[16,3]{0,1:T(4,128)(4,1)S(1)}, pred[16,3]{0,1:T(4,128)(4,1)}, u32[]{:S(2)}) copy-start(pred[16,3]{0,1:T(4,128)(4,1)} %constant.90) | copy-start | bytes 148
  22.3 8.0 %collective-permute-start.2 = (f32[2,4,16,320]{3,1,2,0:T(4,128)S(1)}, f32[2,4,16,320]{3,1,2,0:T(4,128)S(1)}, u32[]{:S(2)}, u32[]{:S(2)}) collective-permute-start(f32[2,4,16,320]{3,1,2,0:T(4,128)S(1)} %get-tuple-element.120), channel_id=1, source_target_pairs={{0,4},{12,8},{1,5},{13,9},{2,6},{14,10},{3,7},{15,11},{16,20},{28,... | collective-permute-start | bytes 491528 | tf_op jit(solution)/shard_map/ppermute | solution.py:101
  27.4 2.7 %copy-start = (bf16[2,320,3,3,320]{4,1,3,2,0:T(8,128)(2,1)}, bf16[2,320,3,3,320]{4,1,3,2,0:T(8,128)(2,1)S(1)}, u32[]{:S(2)}) copy-start(bf16[2,320,3,3,320]{4,1,3,2,0:T(8,128)(2,1)S(1)} %maximum_select_fusion.1) | copy-start | bytes 11059204
  37.7 6.5 %collective-permute-start.3 = (bf16[2,4,16,320]{3,1,2,0:T(4,128)(2,1)S(1)}, bf16[2,4,16,320]{3,1,2,0:T(4,128)(2,1)S(1)}, u32[]{:S(2)}, u32[]{:S(2)}) collective-permute-start(bf16[2,4,16,320]{3,1,2,0:T(4,128)(2,1)S(1)} %fusion.90), channel_id=1, source_target_pairs={{4,0},{8,12},{5,1},{9,13},{6,2},{10,14},{7,3},{11,15},{20,16},{24,... | collective-permute-start | bytes 245768 | tf_op jit(solution)/shard_map/ppermute | solution.py:191
where the time goes:
time: 61.1 us; the launch traced here: 60.7 us
  local copies, waits for them, and re-layouts  20.8 us (34%)
  matrix products  12.3 us (20%)
  blocking collectives  8.79 us (14%)
  other arithmetic  6.47 us (11%)
  waiting for transfers between devices  6.18 us (10%)
  starting transfers between devices  5.49 us (9%)
    all_gather x1, blocking collectives, local(): every = lax.all_gather(both, ('dp', 'mp'), axis=0, tiled=True)  8.79 us
    ppermute x1, waiting for transfers between devices, local(): lax.ppermute(jnp.where(lower, c0, a_last), 'pipe', [(1, 0), (pipe_size -...  5.09 us
    conv_general_dilated x2, matrix products, conv_t(): lax.conv_general_dilated(flipped, weight, (1, 1), ((1, 1), (1, 1)), dimen...  4.76 us
    reshape x1, local copies, waits for them, and re-layouts, local(): return grad.reshape(1, -1)  4.57 us
    another operation x1, local copies, waits for them, and re-layouts, local(): own = lax.optimization_barrier(section_weight[0].reshape(2, chan_half, 9,...  4.47 us
    conv_general_dilated x4, matrix products, conv(): lax.conv_general_dilated(act, weight, (1, 1), ((1, 1), (1, 1)), dimension...  4.36 us
    ppermute x2, starting transfers between devices, up(): return lax.ppermute(v, 'pipe', pairs)  3.68 us
    select_n x1, other arithmetic, local(): jnp.where(lane == 0, jnp.concatenate([own, other], 1), jnp.concatenate([o...  3.6 us
  transfers between devices with their start and end apart: 4, of which 2 were waited for; matrix products, arithmetic and copies ran while one was open for 20% of the time, Pallas kernels for 0%

commit v1 on v0

--- a/solution.py
+++ b/solution.py
@@ -2,6 +2,18 @@
 import jax.numpy as jnp
 from jax import lax
 from jax.sharding import PartitionSpec as P
+
+
+def gather_around(shard, axis, dim):
+    ways, here, step = (lax.axis_size(axis), lax.axis_index(axis), shard.shape[dim])
+    dims = [n * ways if d == dim else n for d, n in enumerate(shard.shape)]
+    full = lax.dynamic_update_slice_in_dim(
+        jnp.zeros(dims, shard.dtype), shard, here * step, axis=dim
+    )
+    for far in range(1, ways):
+        shard = lax.ppermute(shard, axis, [(d, (d + 1) % ways) for d in range(ways)])
+        full = lax.dynamic_update_slice_in_dim(full, shard, (here - far) % ways * step, axis=dim)
+    return full
 
 
 def silu_slope(pre_act):
@@ -198,7 +210,7 @@
     act_sel = jnp.where(lower, acts_lo[stage], acts_up[stage])
     cot_sel = jnp.where(lower, cots_lo[stage], cots_up[stage])
     both = jnp.concatenate([act_sel, cot_sel], axis=-1)
-    every = lax.all_gather(both, ("dp", "mp"), axis=0, tiled=True)
+    every = gather_around(both, ("dp", "mp"), 0)
     act_all = every[..., :channels]
     cot_all = lax.dynamic_slice_in_dim(every, channels + low, chan_half, 3)
     grad = weight_grad(act_all, cot_all)

time: 61.1 us -> 66.9 us (1.095)
  waiting for transfers between devices: 6.18 us -> 19.1 us
  blocking collectives: 8.79 us -> 0 us
  local copies, waits for them, and re-layouts: 20.8 us -> 21.6 us
  matrix products: 12.3 us -> 13 us
    ppermute x0 -> x3, waiting for transfers between devices: none -> 13.3 us  [gather_around(): lax.ppermute(shard, axis, [(d, (d + 1) % ways) for d in range(ways)])]
    all_gather x1 -> x0, blocking collectives: 8.79 us -> none  [local(): every = lax.all_gather(both, ('dp', 'mp'), axis=0, tiled=True)]
    dynamic_update_slice x0 -> x4, local copies, waits for them, and re-layouts: none -> 1.13 us  [the longest x3 0.84 us: gather_around(): lax.dynamic_update_slice_in_dim(full, shard, (here - far) % ways * step,...]
    conv_general_dilated x2, matrix products: 2.28 us -> 3.02 us  [conv_flipped(): lax.conv_general_dilated(flipped, weight, (1, 1), ((1, 1), (1, 1)), dimen...]
    unnamed x11 -> x15, local copies, waits for them, and re-layouts: 2.84 us -> 3.13 us
  transfers between devices with their start and end apart: 4 -> 7, of which waited for: 2 -> 5; matrix products, arithmetic and copies ran while one was open for 20% -> 21% of each run, Pallas kernels for 0% -> 0%
where the time goes in v1:
time: 66.9 us; the launch traced here: 66.6 us
  local copies, waits for them, and re-layouts  21.6 us (32%)
  waiting for transfers between devices  19.1 us (29%)
  matrix products  13 us (19%)
  other arithmetic  6.46 us (10%)
  starting transfers between devices  5.55 us (8%)
    ppermute x3, waiting for transfers between devices, gather_around(): lax.ppermute(shard, axis, [(d, (d + 1) % ways) for d in range(ways)])  13.3 us
    ppermute x1, waiting for transfers between devices, local(): lax.ppermute(jnp.where(lower, c0, a_last), 'pipe', [(1, 0), (pipe_size -...  5.18 us
    conv_general_dilated x2, matrix products, conv_t(): lax.conv_general_dilated(flipped, weight, (1, 1), ((1, 1), (1, 1)), dimen...  4.76 us
    reshape x1, local copies, waits for them, and re-layouts, local(): return grad.reshape(1, -1)  4.57 us
    another operation x1, local copies, waits for them, and re-layouts, local(): own = lax.optimization_barrier(section_weight[0].reshape(2, chan_half, 9,...  4.44 us
    conv_general_dilated x4, matrix products, conv(): lax.conv_general_dilated(act, weight, (1, 1), ((1, 1), (1, 1)), dimension...  4.35 us
    ppermute x2, starting transfers between devices, up(): return lax.ppermute(v, 'pipe', pairs)  3.68 us
    select_n x1, other arithmetic, local(): jnp.where(lane == 0, jnp.concatenate([own, other], 1), jnp.concatenate([o...  3.57 us
  transfers between devices with their start and end apart: 7, of which 5 were waited for; matrix products, arithmetic and copies ran while one was open for 21% of the time, Pallas kernels for 0%

profile of v1, /device:TPU:0, one launch (start us, length us, event | category | flops | bytes accessed | tf_op | source)
XLA Modules:
  0.0 66.6 jit_solution(18442952312014087435)
XLA Ops:
  0.0 2.7 %reshape.100 = bf16[921600]{0:T(1024)(128)(2,1)S(1)} reshape(bf16[1,2,460800]{2,1,0:T(2,128)(2,1)} %param.10) | data formatting | bytes 3686400
  2.7 4.4 %reshape_squeeze.3 = bf16[2,160,9,320]{3,2,1,0:T(8,128)(2,1)} reshape(bf16[921600]{0:T(1024)(128)(2,1)S(1)} %reshape.100) | data formatting | bytes 3686400 | tf_op jit(solution)/shard_map/reshape;squeeze | solution.py:105
  7.1 2.7 %copy.104 = bf16[2,9,160,320]{3,2,1,0:T(8,128)(2,1)S(1)} copy(bf16[2,9,160,320]{3,1,2,0:T(8,128)(2,1)} %bitcast.136) | data formatting | bytes 3686400 | tf_op jit(solution)/shard_map/transpose | solution.py:106
  9.8 0.5 collective-permute-start
  10.4 3.3 %conditional.3 = (f32[2,4,16,160]{3,1,2,0:T(4,128)S(1)}, f32[2,4,16,320]{3,1,2,0:T(4,128)S(1)}) conditional(s32[]{:T(128)} %convert_element_type.83, () %tuple.30, (bf16[2,160,3,3,320]{4,1,3,2,0:T(8,128)(2,1)S(1)}, bf16[2,4,16,320]{3,2,1,0:T(8,128)(2,1)S(1)}, bf16[2,4,16,320]{3,2,1,0:T(8,128)(2,1)S(1)}, s32[]{:T(128)}) %tuple.56), branch_computations={%region_0.1_spmd, %region_1.2_spmd} | conditional | flops 295925760 | bytes 5914438 | solution.py:84
  10.6 0.2 dynamic-slice_bitcast_fusion
  10.9 0.2 fusion.7
  11.1 1.2 %convolution_select_fusion = f32[4,16,3,320]{3,1,2,0:T(8,128)S(1)} fusion(bf16[2,160,3,3,320]{4,1,3,2,0:T(8,128)(2,1)S(1)} %get-tuple-element.56, bf16[4,2,8,5,160]{4,1,3,2,0:T(2,128)(2,1)S(1)} %fusion.7, pred[16,3]{0,1:T(4,128)(4,1)} %constant.125), kind=kOutput, calls=%fused_computation | convolution fusion | flops 147517440 | bytes 1515568 | tf_op jit(solution)/shard_map/cond/branch_1_fun/conv_general_dilated | solution.py:49
  12.8 0.2 fusion.4
  13.0 0.5 convolution_select_fusion.1
  13.6 0.1 copy.97
  13.7 0.7 collective-permute-done
  14.4 2.7 %conditional.4 = (bf16[2,4,16,320]{3,1,2,0:T(4,128)(2,1)S(1)}) conditional(s32[]{:T(128)} %convert_element_type.83, () %tuple.29, (bf16[2,4,16,320]{3,2,1,0:T(8,128)(2,1)S(1)}, s32[]{:T(128)}, bf16[2,160,3,3,320]{4,1,3,2,0:T(8,128)(2,1)}, bf16[2,4,16,320]{3,2,1,0:T(8,128)(2,1)S(1)}, f32[2,4,16,160]{3,1,2,0:T(4,128)S(1)}) %tuple.32), branch_computations={%region_2.3_spmd, %region_3.4_spmd} | conditional | flops 148346880 | bytes 3082772 | solution.py:84
  14.7 0.2 fusion.12
  14.9 1.8 %convolution_select_fusion.2 = f32[4,16,3,160]{3,1,2,0:T(8,128)S(1)} fusion(bf16[2,160,3,3,320]{4,1,3,2,0:T(8,128)(2,1)} %get-tuple-element.63, bf16[4,2,8,5,320]{4,1,3,2,0:T(2,128)(2,1)S(1)} %fusion.12, pred[16,3]{0,1:T(4,128)(4,1)} %constant.124), kind=kOutput, calls=%fused_computation.18 | convolution fusion | flops 147486720 | bytes 1434112 | tf_op jit(solution)/shard_map/cond/branch_1_fun/conv_general_dilated | solution.py:25
  16.9 0.2 fusion.16
  17.1 2.2 %collective-permute-start.1 = (bf16[2,4,16,320]{3,2,1,0:T(8,128)(2,1)S(1)}, bf16[2,4,16,320]{3,2,1,0:T(8,128)(2,1)S(1)}, u32[]{:S(2)}, u32[]{:S(2)}) collective-permute-start(bf16[2,4,16,320]{3,2,1,0:T(8,128)(2,1)S(1)} %copy.109), channel_id=1, source_target_pairs={{0,4},{12,8},{1,5},{13,9},{2,6},{14,10},{3,7},{15,11},{16,20},{28,... | collective-permute-start | bytes 245768 | tf_op jit(solution)/shard_map/ppermute | solution.py:113
  19.3 3.0 %conditional.5 = (f32[2,4,16,320]{3,1,2,0:T(4,128)S(1)}) conditional(s32[]{:T(128)} %convert_element_type.83, () %tuple.33, (bf16[2,4,16,320]{3,2,1,0:T(8,128)(2,1)S(1)}, s32[]{:T(128)}, bf16[2,160,3,3,320]{4,1,3,2,0:T(8,128)(2,1)}, f32[2,4,16,320]{3,1,2,0:T(4,128)S(1)}) %tuple.34), branch_computations={%region_4.5_spmd, %region_5.6_spmd} | conditional | flops 147865600 | bytes 3548744 | solution.py:84
  19.5 0.1 dynamic-slice_bitcast_fusion.1
  19.8 0.2 fusion.20
  20.0 1.8 %convolution_select_fusion.3 = f32[4,16,3,320]{3,1,2,0:T(8,128)S(1)} fusion(bf16[2,160,3,3,320]{4,1,3,2,0:T(8,128)(2,1)} %get-tuple-element.67, bf16[4,2,8,5,160]{4,1,3,2,0:T(2,128)(2,1)S(1)} %fusion.20, pred[16,3]{0,1:T(4,128)(4,1)} %constant.123), kind=kOutput, calls=%fused_computation.30 | convolution fusion | flops 147517440 | bytes 1454592 | tf_op jit(solution)/shard_map/cond/branch_1_fun/conv_general_dilated | solution.py:49
  22.0 0.3 rev.20
  22.3 1.5 %collective-permute-start.2 = (f32[2,4,16,320]{3,2,1,0:T(8,128)S(1)}, f32[2,4,16,320]{3,2,1,0:T(8,128)S(1)}, u32[]{:S(2)}, u32[]{:S(2)}) collective-permute-start(f32[2,4,16,320]{3,2,1,0:T(8,128)S(1)} %copy.111), channel_id=1, source_target_pairs={{0,4},{12,8},{1,5},{13,9},{2,6},{14,10},{3,7},{15,11},{16,20},{28,... | collective-permute-start | bytes 491528 | tf_op jit(solution)/shard_map/ppermute | solution.py:113
  23.8 3.6 %maximum_select_fusion.1 = bf16[2,320,3,3,320]{4,1,3,2,0:T(8,128)(2,1)S(1)} fusion(bf16[2,160,3,3,320]{4,1,3,2,0:T(8,128)(2,1)} %collective-permute-done, bf16[2,160,3,3,320]{4,1,3,2,0:T(8,128)(2,1)S(1)} %bitcast.139, pred[]{:T(512)S(6)} %eq.16), kind=kLoop, calls=%fused_computation.40 | loop fusion | flops 16588800 | bytes 7372801 | tf_op jit(solution)/shard_map/jit(_where)/select_n | solution.py:152
  27.8 0.2 fusion.38
  28.0 1.0 %fusion.29 = f32[4,16,3,320]{3,1,2,0:T(8,128)S(1)} fusion(bf16[2,320,3,3,320]{4,1,3,2,0:T(8,128)(2,1)S(1)} %maximum_select_fusion.1, bf16[4,2,8,5,320]{4,1,3,2,0:T(2,128)(2,1)S(1)} %fusion.38, pred[16,3]{0,1:T(4,128)(4,1)S(1)} %copy-done.3), kind=kOutput, calls=%fused_computation.49 | convolution fusion | flops 294973440 | bytes 2703872 | tf_op jit(solution)/shard_map/conv_general_dilated | solution.py:25
  29.7 0.2 fusion.39
  29.9 1.0 %fusion.27 = f32[4,16,3,320]{3,1,2,0:T(8,128)S(1)} fusion(bf16[2,320,3,3,320]{4,1,3,2,0:T(8,128)(2,1)S(1)} %maximum_select_fusion.1, bf16[4,2,8,5,320]{4,1,3,2,0:T(2,128)(2,1)S(1)} %fusion.39, pred[16,3]{0,1:T(4,128)(4,1)S(1)} %copy-done.3), kind=kOutput, calls=%fused_computation.47 | convolution fusion | flops 294973440 | bytes 2703872 | tf_op jit(solution)/shard_map/conv_general_dilated | solution.py:25
  31.2 0.1 rev.25
  31.7 0.2 fusion.40
  31.9 2.4 %fusion.28 = f32[4,16,3,320]{3,1,2,0:T(8,128)S(1)} fusion(bf16[2,320,3,3,320]{4,1,3,2,0:T(8,128)(2,1)} %copy-done, bf16[4,2,8,5,320]{4,1,3,2,0:T(2,128)(2,1)S(1)} %fusion.40, pred[16,3]{0,1:T(4,128)(4,1)S(1)} %copy-done.3), kind=kOutput, calls=%fused_computation.48 | convolution fusion | flops 294973440 | bytes 2662448 | tf_op jit(solution)/shard_map/conv_general_dilated | solution.py:37
  34.7 0.1 rev.27
  35.1 0.2 fusion.41
  35.4 2.4 %fusion.30 = f32[4,16,3,320]{3,1,2,0:T(8,128)S(1)} fusion(bf16[2,320,3,3,320]{4,1,3,2,0:T(8,128)(2,1)} %copy-done, bf16[4,2,8,5,320]{4,1,3,2,0:T(2,128)(2,1)S(1)} %fusion.41, pred[16,3]{0,1:T(4,128)(4,1)S(1)} %copy-done.3), kind=kOutput, calls=%fused_computation.50 | convolution fusion | flops 294973440 | bytes 2662448 | tf_op jit(solution)/shard_map/conv_general_dilated | solution.py:37
  38.0 0.2 fusion.75
  38.2 1.3 %collective-permute-start.3 = (bf16[2,4,16,320]{3,2,1,0:T(8,128)(2,1)S(1)}, bf16[2,4,16,320]{3,2,1,0:T(8,128)(2,1)S(1)}, u32[]{:S(2)}, u32[]{:S(2)}) collective-permute-start(bf16[2,4,16,320]{3,2,1,0:T(8,128)(2,1)S(1)} %fusion.75), channel_id=1, source_target_pairs={{4,0},{8,12},{5,1},{9,13},{6,2},{10,14},{7,3},{11,15},{20,16},{24,... | collective-permute-start | bytes 245768 | tf_op jit(solution)/shard_map/ppermute | solution.py:203
  39.5 5.2 %collective-permute-done.3 = bf16[2,4,16,320]{3,2,1,0:T(8,128)(2,1)S(1)} collective-permute-done((bf16[2,4,16,320]{3,2,1,0:T(8,128)(2,1)S(1)}, bf16[2,4,16,320]{3,2,1,0:T(8,128)(2,1)S(1)}, u32[]{:S(2)}, u32[]{:S(2)}) %collective-permute-start.3) | collective-permute-done | bytes 81952 | tf_op jit(solution)/shard_map/ppermute | solution.py:203
  44.7 0.2 fusion.82
  45.1 0.3 copy_dynamic-update-slice_fusion.3
  45.4 4.4 %collective-permute-done.4 = bf16[2,4,16,640]{3,2,1,0:T(8,128)(2,1)S(1)} collective-permute-done((bf16[2,4,16,640]{3,2,1,0:T(8,128)(2,1)S(1)}, bf16[2,4,16,640]{3,2,1,0:T(8,128)(2,1)S(1)}, u32[]{:S(2)}, u32[]{:S(2)}) %collective-permute-start.4) | collective-permute-done | bytes 163872 | tf_op jit(solution)/shard_map/ppermute | solution.py:14
  49.8 0.3 copy_dynamic-update-slice_fusion.2
  50.1 4.5 %collective-permute-done.5 = bf16[2,4,16,640]{3,2,1,0:T(8,128)(2,1)S(1)} collective-permute-done((bf16[2,4,16,640]{3,2,1,0:T(8,128)(2,1)S(1)}, bf16[2,4,16,640]{3,2,1,0:T(8,128)(2,1)S(1)}, u32[]{:S(2)}, u32[]{:S(2)}) %collective-permute-start.5) | collective-permute-done | bytes 163872 | tf_op jit(solution)/shard_map/ppermute | solution.py:14
  54.5 0.3 copy_dynamic-update-slice_fusion.1
  54.8 4.5 %collective-permute-done.6 = bf16[2,4,16,640]{3,2,1,0:T(8,128)(2,1)S(1)} collective-permute-done((bf16[2,4,16,640]{3,2,1,0:T(8,128)(2,1)S(1)}, bf16[2,4,16,640]{3,2,1,0:T(8,128)(2,1)S(1)}, u32[]{:S(2)}, u32[]{:S(2)}) %collective-permute-start.6) | collective-permute-done | bytes 163872 | tf_op jit(solution)/shard_map/ppermute | solution.py:14
  59.3 0.3 copy_dynamic-update-slice_fusion
  59.6 0.9 %fusion.35 = f32[160,3,3,320]{3,0,2,1:T(8,128)S(1)} fusion(bf16[8,4,16,640]{3,0,2,1:T(8,128)(2,1)S(1)} %copy_dynamic-update-slice_fusion, s32[]{:T(128)S(6)} %select_n.105), kind=kOutput, calls=%fused_computation.56 | convolution fusion | flops 376832000 | bytes 2498564 | tf_op jit(solution)/shard_map/conv_general_dilated | solution.py:60
  60.5 1.5 %copy.132 = f32[160,3,3,320]{3,2,1,0:T(4,128)S(1)} copy(f32[160,3,3,320]{3,0,2,1:T(8,128)S(1)} %fusion.35) | data formatting | bytes 3686400 | tf_op jit(solution)/shard_map/conv_general_dilated | solution.py:60
  62.0 4.6 %reshape.19 = f32[1,460800]{1,0:T(1,128)} reshape(f32[160,3,3,320]{3,2,1,0:T(4,128)S(1)} %copy.132) | data formatting | bytes 3686400 | tf_op jit(solution)/shard_map/reshape | solution.py:217
  (72 shorter events, 4.3 us)
Async XLA Ops:
  7.1 3.2 %copy-start.1 = (bf16[1,2,2,4,16,320]{5,4,3,2,1,0:T(8,128)(2,1)S(1)}, bf16[1,2,2,4,16,320]{5,4,3,2,1,0:T(8,128)(2,1)}, u32[]{:S(2)}) copy-start(bf16[1,2,2,4,16,320]{5,4,3,2,1,0:T(8,128)(2,1)} %param.11) | copy-start | bytes 491524
  7.1 3.2 %copy-start.2 = (bf16[1,2,2,4,16,320]{5,4,3,2,1,0:T(8,128)(2,1)S(1)}, bf16[1,2,2,4,16,320]{5,4,3,2,1,0:T(8,128)(2,1)}, u32[]{:S(2)}) copy-start(bf16[1,2,2,4,16,320]{5,4,3,2,1,0:T(8,128)(2,1)} %param.9) | copy-start | bytes 491524
  9.8 4.6 %collective-permute-start = (bf16[2,160,3,3,320]{4,1,3,2,0:T(8,128)(2,1)S(1)}, bf16[2,160,3,3,320]{4,1,3,2,0:T(8,128)(2,1)}, u32[]{:S(2)}, u32[]{:S(2)}) collective-permute-start(bf16[2,160,3,3,320]{4,1,3,2,0:T(8,128)(2,1)S(1)} %bitcast.137), channel_id=1, source_target_pairs={{0,1},{1,0},{2,3},{3,2},{4,5},{5,4},{6,7},{7,6},{8,9},{9,8},{10,11... | collective-permute-start | bytes 5529608 | tf_op jit(solution)/shard_map/ppermute | solution.py:109
  11.1 1.9 %copy-start.4 = (pred[16,3]{0,1:T(4,128)(4,1)S(1)}, pred[16,3]{0,1:T(4,128)(4,1)}, u32[]{:S(2)}) copy-start(pred[16,3]{0,1:T(4,128)(4,1)} %constant.125) | copy-start | bytes 148 | tf_op jit(solution)/shard_map/cond
  17.1 10.3 %collective-permute-start.1 = (bf16[2,4,16,320]{3,2,1,0:T(8,128)(2,1)S(1)}, bf16[2,4,16,320]{3,2,1,0:T(8,128)(2,1)S(1)}, u32[]{:S(2)}, u32[]{:S(2)}) collective-permute-start(bf16[2,4,16,320]{3,2,1,0:T(8,128)(2,1)S(1)} %copy.109), channel_id=1, source_target_pairs={{0,4},{12,8},{1,5},{13,9},{2,6},{14,10},{3,7},{15,11},{16,20},{28,... | collective-permute-start | bytes 245768 | tf_op jit(solution)/shard_map/ppermute | solution.py:113
  22.3 5.7 %copy-start.3 = (pred[16,3]{0,1:T(4,128)(4,1)S(1)}, pred[16,3]{0,1:T(4,128)(4,1)}, u32[]{:S(2)}) copy-start(pred[16,3]{0,1:T(4,128)(4,1)} %constant.119) | copy-start | bytes 148
  22.3 8.7 %collective-permute-start.2 = (f32[2,4,16,320]{3,2,1,0:T(8,128)S(1)}, f32[2,4,16,320]{3,2,1,0:T(8,128)S(1)}, u32[]{:S(2)}, u32[]{:S(2)}) collective-permute-start(f32[2,4,16,320]{3,2,1,0:T(8,128)S(1)} %copy.111), channel_id=1, source_target_pairs={{0,4},{12,8},{1,5},{13,9},{2,6},{14,10},{3,7},{15,11},{16,20},{28,... | collective-permute-start | bytes 491528 | tf_op jit(solution)/shard_map/ppermute | solution.py:113
  27.4 2.5 %copy-start = (bf16[2,320,3,3,320]{4,1,3,2,0:T(8,128)(2,1)}, bf16[2,320,3,3,320]{4,1,3,2,0:T(8,128)(2,1)S(1)}, u32[]{:S(2)}) copy-start(bf16[2,320,3,3,320]{4,1,3,2,0:T(8,128)(2,1)S(1)} %maximum_select_fusion.1) | copy-start | bytes 11059204
  38.2 6.5 %collective-permute-start.3 = (bf16[2,4,16,320]{3,2,1,0:T(8,128)(2,1)S(1)}, bf16[2,4,16,320]{3,2,1,0:T(8,128)(2,1)S(1)}, u32[]{:S(2)}, u32[]{:S(2)}) collective-permute-start(bf16[2,4,16,320]{3,2,1,0:T(8,128)(2,1)S(1)} %fusion.75), channel_id=1, source_target_pairs={{4,0},{8,12},{5,1},{9,13},{6,2},{10,14},{7,3},{11,15},{20,16},{24,... | collective-permute-start | bytes 245768 | tf_op jit(solution)/shard_map/ppermute | solution.py:203
  45.0 4.8 %collective-permute-start.4 = (bf16[2,4,16,640]{3,2,1,0:T(8,128)(2,1)S(1)}, bf16[2,4,16,640]{3,2,1,0:T(8,128)(2,1)S(1)}, u32[]{:S(2)}, u32[]{:S(2)}) collective-permute-start(bf16[2,4,16,640]{3,2,1,0:T(8,128)(2,1)S(1)} %pad_maximum_fusion), channel_id=1, source_target_pairs={{0,1},{1,2},{2,3},{3,0},{4,5},{5,6},{6,7},{7,4},{8,9},{9,10},{10,1... | collective-permute-start | bytes 491528 | tf_op jit(solution)/shard_map/ppermute | solution.py:14
  49.8 4.7 %collective-permute-start.5 = (bf16[2,4,16,640]{3,2,1,0:T(8,128)(2,1)S(1)}, bf16[2,4,16,640]{3,2,1,0:T(8,128)(2,1)S(1)}, u32[]{:S(2)}, u32[]{:S(2)}) collective-permute-start(bf16[2,4,16,640]{3,2,1,0:T(8,128)(2,1)S(1)} %collective-permute-done.4), channel_id=1, source_target_pairs={{0,1},{1,2},{2,3},{3,0},{4,5},{5,6},{6,7},{7,4},{8,9},{9,10},{10,1... | collective-permute-start | bytes 491528 | tf_op jit(solution)/shard_map/ppermute | solution.py:14
  54.5 4.7 %collective-permute-start.6 = (bf16[2,4,16,640]{3,2,1,0:T(8,128)(2,1)S(1)}, bf16[2,4,16,640]{3,2,1,0:T(8,128)(2,1)S(1)}, u32[]{:S(2)}, u32[]{:S(2)}) collective-permute-start(bf16[2,4,16,640]{3,2,1,0:T(8,128)(2,1)S(1)} %collective-permute-done.5), channel_id=1, source_target_pairs={{0,1},{1,2},{2,3},{3,0},{4,5},{5,6},{6,7},{7,4},{8,9},{9,10},{10,1... | collective-permute-start | bytes 491528 | tf_op jit(solution)/shard_map/ppermute | solution.py:14
